TPU v7x, 128 devices: a whole 4x4x4 slice. The times are simulated.
128 devices in a mesh: tm: 64 (over x, z, y_lo, core), row: 2 (over y_hi).
Axes of the slice: x: 4, y: 4 (y_hi: 2, y_lo: 2; y = y_hi * 2 + y_lo), z: 4, core: 2. Of those that a mesh axis runs over, the one named last changes fastest.
Arguments:
- slice_ops: bfloat16 [64, 2048, 2048], P('tm', 'row'), may hold values from -6 to 6
- base_op: bfloat16 [2048, 2048], replicated, may hold values from -6 to 6
- load_table: float32 [16, 2048], replicated, may hold values from -1 to 1
- phase_idx: int32 [64, 2], P('tm'), may hold values from 0 to 15
- step_counts: int32 [64, 2], P('tm'), may hold values from 1 to 8
Outputs:
- windows: bfloat16 [64, 2048, 2048], P('tm', 'row')
All inputs are finite; a program needn't handle non-finite values.
Results may differ from a plain program's by a relative error of at most 0.012.
Values may be sent and summed in bfloat16 or wider, within the bound.
No kernel may reach another device: no remote copies, remote signals or barrier semaphores. Data moves between devices by JAX's collectives and lax.ppermute only.
A program may use at most 128 MiB of HBM per device.

v0:
```python
import math
import jax
import jax.numpy as jnp
from jax import lax
from jax.sharding import PartitionSpec as P

LEVELS = 2


def shifted(value, axis, steps):
    count = lax.axis_size(axis)
    pairs = [(source, (source + steps) % count) for source in range(count)]
    return lax.ppermute(value, axis, pairs)


def shards(slice_ops, base_op, load_table, phase_idx, step_counts):
    state_size = base_op.shape[0]
    norm_scale = 1.0 / math.sqrt(state_size)
    phase_count = load_table.shape[0]
    index_row = phase_idx[0]
    count_row = step_counts[0].astype(jnp.float32)
    one_hot = (
        index_row[:, None] == lax.broadcasted_iota(jnp.int32, (index_row.shape[0], phase_count), 1)
    ).astype(jnp.float32)
    table_rows = jnp.dot(one_hot, load_table, precision=lax.Precision.HIGHEST)
    gain_rows = jnp.exp(0.1 * count_row[:, None] * table_rows)
    right_factor = (base_op * gain_rows[0]).astype(jnp.bfloat16)
    left_factor = (slice_ops[0] * gain_rows[1]).astype(jnp.bfloat16)
    product = jnp.dot(left_factor, right_factor, preferred_element_type=jnp.float32)
    current = (product * norm_scale).astype(jnp.bfloat16)
    for depth_level in range(LEVELS):
        distance = 2**depth_level
        whole = lax.all_gather(current, "row", axis=0, tiled=True)
        earlier = shifted(whole, "tm", distance)
        combined = jnp.dot(current, earlier, preferred_element_type=jnp.float32)
        current = (combined * norm_scale).astype(jnp.bfloat16)
    return current[None]


def solution(mesh):
    return jax.shard_map(
        shards,
        mesh=mesh,
        in_specs=(P("tm", "row", None), P(), P(), P("tm", None), P("tm", None)),
        out_specs=P("tm", "row", None),
        check_vma=False,
    )
```

profile of v0, /device:TPU:0, one launch (start us, length us, event | category | flops | bytes accessed | tf_op | source)
XLA Modules:
  0.0 551.6 jit_solution(3729319134731721616)
XLA Ops:
  6.5 0.0 copy-start
  6.5 0.0 all-gather.3.cloned.1.call-start
  6.5 0.7 multiply_bitcast_fusion
  7.2 0.2 copy-done
  7.5 0.9 fusion.7
  8.4 13.8 %multiply_convert_fusion.4 = bf16[1024,2048]{1,0:T(8,128)(2,1)} fusion(bf16[2048,2048]{1,0:T(8,128)(2,1)} %param.6, f32[2048]{0:T(1024)S(1)} %bitcast.19, bf16[1,1024,2048]{2,1,0:T(8,128)(2,1)} %param.5, f32[2048]{0:T(1024)S(1)} %bitcast.18), kind=kOutput, calls=%fused_computation.6 | convolution fusion | flops 8613003264 | bytes 16793600 | tf_op jit(solution)/shard_map/dot_general | solution.py:29
  22.2 0.0 all-gather.3.cloned.1.call-update
  22.2 0.0 all-gather.5.cloned.1.call-start
  22.3 110.6 %all-gather.3.cloned.1.call-done = bf16[2048,2048]{1,0:T(8,128)(2,1)} async-done(((bf16[1024,2048]{1,0:T(8,128)(2,1)}), bf16[2048,2048]{1,0:T(8,128)(2,1)}) %all-gather.3.cloned.1.call-update) | async-done | bytes 8388624 | tf_op jit(solution)/shard_map/all_gather | solution.py:33
  132.9 0.0 collective-permute-start
  132.9 97.3 %collective-permute-done = bf16[2048,2048]{1,0:T(8,128)(2,1)S(1)} collective-permute-done((bf16[2048,2048]{1,0:T(8,128)(2,1)}, bf16[2048,2048]{1,0:T(8,128)(2,1)S(1)}, u32[]{:S(2)}, u32[]{:S(2)}) %collective-permute-start) | collective-permute-done | bytes 8388640 | tf_op jit(solution)/shard_map/ppermute | solution.py:13
  230.2 12.1 %multiply_convert_fusion.3 = bf16[1024,2048]{1,0:T(8,128)(2,1)} fusion(bf16[1024,2048]{1,0:T(8,128)(2,1)} %multiply_convert_fusion.4, bf16[2048,2048]{1,0:T(8,128)(2,1)S(1)} %collective-permute-done), kind=kOutput, calls=%fused_computation.5 | convolution fusion | flops 8594128896 | bytes 16777216 | tf_op jit(solution)/shard_map/dot_general | solution.py:35
  242.3 0.0 all-gather.5.cloned.1.call-update
  242.4 103.7 %all-gather.5.cloned.1.call-done = bf16[2048,2048]{1,0:T(8,128)(2,1)} async-done(((bf16[1024,2048]{1,0:T(8,128)(2,1)}), bf16[2048,2048]{1,0:T(8,128)(2,1)}) %all-gather.5.cloned.1.call-update) | async-done | bytes 8388624 | tf_op jit(solution)/shard_map/all_gather | solution.py:33
  346.1 0.6 collective-permute-start.1
  346.7 186.0 %collective-permute-done.1 = bf16[2048,2048]{1,0:T(8,128)(2,1)S(1)} collective-permute-done((bf16[2048,2048]{1,0:T(8,128)(2,1)}, bf16[2048,2048]{1,0:T(8,128)(2,1)S(1)}, u32[]{:S(2)}, u32[]{:S(2)}) %collective-permute-start.1) | collective-permute-done | bytes 8388640 | tf_op jit(solution)/shard_map/ppermute | solution.py:13
  532.7 12.1 %fusion.6 = bf16[1,1024,2048]{2,1,0:T(8,128)(2,1)} fusion(bf16[1024,2048]{1,0:T(8,128)(2,1)} %multiply_convert_fusion.3, bf16[2048,2048]{1,0:T(8,128)(2,1)S(1)} %collective-permute-done.1), kind=kOutput, calls=%fused_computation.10 | convolution fusion | flops 8594128896 | bytes 16777216 | tf_op jit(solution)/shard_map/dot_general | solution.py:35
  (1 shorter events, 0.0 us)
Async XLA Ops:
  6.5 0.9 copy-start
  6.5 126.4 %all-gather.3.cloned.1.call-start = ((), (), s32[]{:S(2)}) async-start(), calls=%async_computation | async-start | bytes 12582912 | tf_op jit(solution)/shard_map/all_gather | solution.py:33
  22.2 323.8 %all-gather.5.cloned.1.call-start = ((), (), s32[]{:S(2)}) async-start(), calls=%async_computation.1 | async-start | bytes 12582912 | tf_op jit(solution)/shard_map/all_gather | solution.py:33
  132.9 97.3 %collective-permute-start = (bf16[2048,2048]{1,0:T(8,128)(2,1)}, bf16[2048,2048]{1,0:T(8,128)(2,1)S(1)}, u32[]{:S(2)}, u32[]{:S(2)}) collective-permute-start(bf16[2048,2048]{1,0:T(8,128)(2,1)} %all-gather.3.cloned.1.call-done), channel_id=1, source_target_pairs={{0,2},{2,4},{4,6},{6,8},{8,10},{10,12},{12,14},{14,16},{16,18},{18... | collective-permute-start | bytes 25165832 | tf_op jit(solution)/shard_map/ppermute | solution.py:13
  346.1 186.6 %collective-permute-start.1 = (bf16[2048,2048]{1,0:T(8,128)(2,1)}, bf16[2048,2048]{1,0:T(8,128)(2,1)S(1)}, u32[]{:S(2)}, u32[]{:S(2)}) collective-permute-start(bf16[2048,2048]{1,0:T(8,128)(2,1)} %all-gather.5.cloned.1.call-done), channel_id=1, source_target_pairs={{0,4},{2,6},{4,8},{6,10},{8,12},{10,14},{12,16},{14,18},{16,20},{1... | collective-permute-start | bytes 25165832 | tf_op jit(solution)/shard_map/ppermute | solution.py:13
Sparse Core Ops, SparseCore 0:
  22.3 110.5 all-gather.2
  242.5 103.5 all-gather.4
where the time goes:
time: 552 us
  waiting for transfers between devices  498 us (90%)
  matrix products  38.9 us (7%)
  between operations  13.4 us (2%)
    ppermute x2, waiting for transfers between devices, shifted(): return lax.ppermute(value, axis, pairs)  283 us
    all_gather x2, waiting for transfers between devices, shards(): whole = lax.all_gather(current, 'row', axis=0, tiled=True)  214 us
    dot_general x2, matrix products, shards(): combined = jnp.dot(current, earlier, preferred_element_type=jnp.float32)  24.2 us
    dot_general x1, matrix products, shards(): jnp.dot(left_factor, right_factor, preferred_element_type=jnp.float32)  13.8 us
  transfers between devices with their start and end apart: 4, of which 4 were waited for; matrix products, arithmetic and copies ran while one was open for 0% of the time, Pallas kernels for 0%

commit v1 on v0

--- a/solution.py
+++ b/solution.py
@@ -30,7 +30,9 @@
     current = (product * norm_scale).astype(jnp.bfloat16)
     for depth_level in range(LEVELS):
         distance = 2**depth_level
-        whole = lax.all_gather(current, "row", axis=0, tiled=True)
+        whole = jnp.concatenate(
+            lax.all_to_all(jnp.stack([current] * lax.axis_size("row")), "row", 0, 0), axis=0
+        )
         earlier = shifted(whole, "tm", distance)
         combined = jnp.dot(current, earlier, preferred_element_type=jnp.float32)
         current = (combined * norm_scale).astype(jnp.bfloat16)

time: 552 us -> 523 us (0.947)
  waiting for transfers between devices: 498 us -> 281 us
  blocking collectives: 0 us -> 193 us
  between operations: 13.4 us -> 0.03 us
  other arithmetic: 0.69 us -> 12.1 us
    all_gather x2 -> x0, waiting for transfers between devices: 214 us -> none  [shards(): whole = lax.all_gather(current, 'row', axis=0, tiled=True)]
    all_to_all x0 -> x2, blocking collectives: none -> 193 us  [shards(): lax.all_to_all(jnp.stack([current] * lax.axis_size('row')), 'row', 0, 0)]
    another operation x0 -> x2, other arithmetic: none -> 11.4 us  [shards(): jnp.stack([current] * lax.axis_size('row'))]
  transfers between devices with their start and end apart: 4 -> 2, of which waited for: 4 -> 2; matrix products, arithmetic and copies ran while one was open for 0% -> 0% of each run, Pallas kernels for 0% -> 0%
where the time goes in v1:
time: 523 us; the launch traced here: 522 us
  waiting for transfers between devices  281 us (54%)
  blocking collectives  193 us (37%)
  matrix products  34.1 us (7%)
  other arithmetic  12.1 us (2%)
    ppermute x2, waiting for transfers between devices, shifted(): return lax.ppermute(value, axis, pairs)  281 us
    all_to_all x2, blocking collectives, shards(): lax.all_to_all(jnp.stack([current] * lax.axis_size('row')), 'row', 0, 0)  193 us
    dot_general x2, matrix products, shards(): combined = jnp.dot(current, earlier, preferred_element_type=jnp.float32)  20.7 us
    dot_general x1, matrix products, shards(): jnp.dot(left_factor, right_factor, preferred_element_type=jnp.float32)  12.5 us
    another operation x2, other arithmetic, shards(): jnp.stack([current] * lax.axis_size('row'))  11.4 us
  transfers between devices with their start and end apart: 2, of which 2 were waited for; matrix products, arithmetic and copies ran while one was open for 0% of the time, Pallas kernels for 0%

profile of v1, /device:TPU:0, one launch (start us, length us, event | category | flops | bytes accessed | tf_op | source)
XLA Modules:
  0.0 522.5 jit_solution(493263166934882879)
XLA Ops:
  0.0 0.0 copy-start
  0.0 0.7 multiply_bitcast_fusion
  0.7 0.2 copy-done
  0.9 0.9 fusion.7
  1.8 12.5 %multiply_convert_fusion.4 = bf16[1024,2048]{1,0:T(8,128)(2,1)S(1)} fusion(bf16[2048,2048]{1,0:T(8,128)(2,1)} %param.6, f32[2048]{0:T(1024)S(1)} %bitcast.27, bf16[1,1024,2048]{2,1,0:T(8,128)(2,1)} %param.5, f32[2048]{0:T(1024)S(1)} %bitcast.26), kind=kOutput, calls=%fused_computation.8 | convolution fusion | flops 8613003264 | bytes 16793600 | tf_op jit(solution)/shard_map/dot_general | solution.py:29
  14.4 4.0 pad_maximum_fusion
  18.3 98.8 %all_to_all.10 = bf16[2,1024,2048]{2,1,0:T(8,128)(2,1)S(1)} all-to-all(bf16[2,1024,2048]{2,1,0:T(8,128)(2,1)} %pad_maximum_fusion), channel_id=1, replica_groups=mesh['tm'=64,'row'=2] {'row'}, dimensions={0} | all-to-all | bytes 16777216 | tf_op jit(solution)/shard_map/all_to_all | solution.py:34
  117.1 0.0 collective-permute-start
  117.1 97.1 %collective-permute-done = bf16[2048,2048]{1,0:T(8,128)(2,1)S(1)} collective-permute-done((bf16[2048,2048]{1,0:T(8,128)(2,1)S(1)}, bf16[2048,2048]{1,0:T(8,128)(2,1)S(1)}, u32[]{:S(2)}, u32[]{:S(2)}) %collective-permute-start) | collective-permute-done | bytes 8388640 | tf_op jit(solution)/shard_map/ppermute | solution.py:13
  214.2 10.4 %multiply_convert_fusion.3 = bf16[1024,2048]{1,0:T(8,128)(2,1)} fusion(bf16[1024,2048]{1,0:T(8,128)(2,1)S(1)} %multiply_convert_fusion.4, bf16[2048,2048]{1,0:T(8,128)(2,1)S(1)} %collective-permute-done), kind=kOutput, calls=%fused_computation.7 | convolution fusion | flops 8594128896 | bytes 16777216 | tf_op jit(solution)/shard_map/dot_general | solution.py:37
  224.5 7.5 %pad_maximum_fusion.1 = bf16[2,1024,2048]{2,1,0:T(8,128)(2,1)} fusion(bf16[1,1024,2048]{2,1,0:T(8,128)(2,1)} %bitcast.25), kind=kLoop, calls=%fused_computation.3 | loop fusion | flops 4194304 | bytes 12582912 | tf_op jit(solution)/shard_map/stack | solution.py:34
  232.0 0.0 copy-start.2
  232.0 94.2 %all_to_all.11 = bf16[2,1024,2048]{2,1,0:T(8,128)(2,1)S(1)} all-to-all(bf16[2,1024,2048]{2,1,0:T(8,128)(2,1)} %pad_maximum_fusion.1), channel_id=1, replica_groups=mesh['tm'=64,'row'=2] {'row'}, dimensions={0} | all-to-all | bytes 16777216 | tf_op jit(solution)/shard_map/all_to_all | solution.py:34
  326.2 1.8 collective-permute-start.1
  328.0 184.1 %collective-permute-done.1 = bf16[2048,2048]{1,0:T(8,128)(2,1)S(1)} collective-permute-done((bf16[2048,2048]{1,0:T(8,128)(2,1)S(1)}, bf16[2048,2048]{1,0:T(8,128)(2,1)S(1)}, u32[]{:S(2)}, u32[]{:S(2)}) %collective-permute-start.1) | collective-permute-done | bytes 8388640 | tf_op jit(solution)/shard_map/ppermute | solution.py:13
  512.1 0.0 copy-done.2
  512.1 0.0 copy-start.1
  512.1 10.4 %fusion.6 = bf16[1,1024,2048]{2,1,0:T(8,128)(2,1)} fusion(bf16[1024,2048]{1,0:T(8,128)(2,1)S(1)} %copy-done.2, bf16[2048,2048]{1,0:T(8,128)(2,1)S(1)} %collective-permute-done.1), kind=kOutput, calls=%fused_computation.12 | convolution fusion | flops 8594128896 | bytes 16777216 | tf_op jit(solution)/shard_map/dot_general | solution.py:37
  522.5 0.0 copy-done.1
  (1 shorter events, 0.0 us)
Async XLA Ops:
  0.0 0.9 copy-start
  117.1 97.1 %collective-permute-start = (bf16[2048,2048]{1,0:T(8,128)(2,1)S(1)}, bf16[2048,2048]{1,0:T(8,128)(2,1)S(1)}, u32[]{:S(2)}, u32[]{:S(2)}) collective-permute-start(bf16[2048,2048]{1,0:T(8,128)(2,1)S(1)} %bitcast.22), channel_id=1, source_target_pairs={{0,2},{2,4},{4,6},{6,8},{8,10},{10,12},{12,14},{14,16},{16,18},{18... | collective-permute-start | bytes 25165832 | tf_op jit(solution)/shard_map/ppermute | solution.py:13
  232.0 280.1 %copy-start.2 = (bf16[1024,2048]{1,0:T(8,128)(2,1)S(1)}, bf16[1024,2048]{1,0:T(8,128)(2,1)}, u32[]{:S(2)}) copy-start(bf16[1024,2048]{1,0:T(8,128)(2,1)} %multiply_convert_fusion.3) | copy-start | bytes 12582916
  326.2 185.9 %collective-permute-start.1 = (bf16[2048,2048]{1,0:T(8,128)(2,1)S(1)}, bf16[2048,2048]{1,0:T(8,128)(2,1)S(1)}, u32[]{:S(2)}, u32[]{:S(2)}) collective-permute-start(bf16[2048,2048]{1,0:T(8,128)(2,1)S(1)} %bitcast.23), channel_id=1, source_target_pairs={{0,4},{2,6},{4,8},{6,10},{8,12},{10,14},{12,16},{14,18},{16,20},{1... | collective-permute-start | bytes 25165832 | tf_op jit(solution)/shard_map/ppermute | solution.py:13
  512.1 10.4 %copy-start.1 = (f32[16,2048]{1,0:T(8,128)S(1)}, f32[16,2048]{1,0:T(8,128)}, u32[]{:S(2)}) copy-start(f32[16,2048]{1,0:T(8,128)} %param.7) | copy-start | bytes 393220
